TPU v7x, 512 devices: a whole 4x8x8 slice. The times are simulated.
512 devices in a mesh: dp: 16 (over z_hi, y), tensor: 32 (over x, z_lo, core).
Axes of the slice: x: 4, y: 8, z: 8 (z_hi: 2, z_lo: 4; z = z_hi * 4 + z_lo), core: 2. Of those that a mesh axis runs over, the one named last changes fastest.
Arguments:
- suffix_states: bfloat16 [32, 128, 2048], P(None, 'dp', 'tensor'), may hold values from -16 to 16
- suffix_lengths: int32 [32], replicated, may hold values from 1 to 128, 2560 in all
- request_group: int32 [32, 1], replicated, may hold values from 0 to 15
- group_owner: int32 [16], replicated, may hold values from 0 to 15, each once
- request_order: int32 [32], replicated, may hold values from 0 to 31, each once
- prefix_cache: bfloat16 [16, 256, 1024], P('dp', 'tensor'), may hold values from -700 to 700
- norm_attn: bfloat16 [2048], replicated, may hold values from 0.099609375 to 1.8984375
- w_query: bfloat16 [2048, 2048], P(None, 'tensor'), may hold values from -0.125 to 0.125
- w_key: bfloat16 [2048, 512], P(None, 'tensor'), may hold values from -0.125 to 0.125
- w_value: bfloat16 [2048, 512], P(None, 'tensor'), may hold values from -0.125 to 0.125
- w_out: bfloat16 [2048, 2048], P('tensor'), may hold values from -0.25 to 0.25
- norm_mlp: bfloat16 [2048], replicated, may hold values from 0.099609375 to 1.8984375
- w_gate: bfloat16 [2048, 8192], P(None, 'tensor'), may hold values from -0.125 to 0.125
- w_up: bfloat16 [2048, 8192], P(None, 'tensor'), may hold values from -0.125 to 0.125
- w_down: bfloat16 [8192, 2048], P('tensor'), may hold values from -0.125 to 0.125
Outputs:
- hidden_out: bfloat16 [32, 128, 2048], P(None, 'dp', 'tensor')
- suffix_keys: bfloat16 [32, 128, 512], P('dp', None, 'tensor')
- suffix_values: bfloat16 [32, 128, 512], P('dp', None, 'tensor')
Inputs may be any that keep to these rules, and one draw needn't show every extreme that they name: `suffix_lengths`: the lengths sum to 2560 and some request has exactly 128. `request_group`: every group has at least one request. `group_owner`: A permutation of the 16 groups onto the slots of prefix_cache. `request_order`: A permutation of the requests; slot s belongs to index s // 2 of dp.
All inputs are finite; a program needn't handle non-finite values.
Results may differ from a plain program's by a relative error of at most 0.03.
Values may be sent and summed in bfloat16 or wider, within the bound.
No kernel may reach another device: no remote copies, remote signals or barrier semaphores. Data moves between devices by JAX's collectives and lax.ppermute only.
A program may use at most 64 MiB of HBM per device.

v0:
```python
import jax
import jax.numpy as jnp
import numpy as np
from jax import lax
from jax.sharding import PartitionSpec as P

H = 32
KVH = 8
HD = 64
L_MAX = 128
P_SIZE = 256
THETA = 10000000.0
EPSILON = 1e-05


def rms_scale(states, gain):
    wide = states.astype(jnp.float32)
    mean_square = jnp.mean(wide * wide, axis=-1, keepdims=True)
    return (wide * lax.rsqrt(mean_square + EPSILON) * gain.astype(jnp.float32)).astype(jnp.bfloat16)


def rotate(vectors, positions):
    half = HD // 2
    freqs = THETA ** (-(jnp.arange(half, dtype=jnp.float32) * 2.0 / HD))
    angles = positions[:, None] * freqs[None, :]
    cosine = jnp.cos(angles)[:, None, :]
    sine = jnp.sin(angles)[:, None, :]
    first = vectors[..., :half]
    second = vectors[..., half:]
    return jnp.concatenate(
        [first * cosine - second * sine, second * cosine + first * sine], axis=-1
    )


def absorb_block(state_now, scores, allowed, value_rows):
    running_max, running_sum, numerator = state_now
    block_max = jnp.max(jnp.where(allowed, scores, -1e30), axis=2)
    new_max = jnp.maximum(running_max, block_max)
    rescale = jnp.exp(running_max - new_max)
    weights = jnp.where(allowed, jnp.exp(scores - new_max[:, :, None]), 0.0)
    running_sum = running_sum * rescale + jnp.sum(weights, axis=2)
    numerator = numerator * rescale[:, :, None] + jnp.einsum(
        "htk,khd->htd", weights.astype(jnp.bfloat16), value_rows, preferred_element_type=jnp.float32
    )
    return (new_max, running_sum, numerator)


def shards(
    suffix_states,
    suffix_lengths,
    request_group,
    group_owner,
    request_order,
    prefix_cache,
    norm_attn,
    w_query,
    w_key,
    w_value,
    w_out,
    norm_mlp,
    w_gate,
    w_up,
    w_down,
):
    dp_count = lax.axis_size("dp")
    tp_count = lax.axis_size("tensor")
    dp_index = lax.axis_index("dp")
    tp_index = lax.axis_index("tensor")
    total_reqs = suffix_lengths.shape[0]
    local_reqs = total_reqs // dp_count
    row_count = local_reqs * L_MAX
    heads_here = w_query.shape[1] // HD
    group_size = H // KVH
    kv_here = max(1, heads_here // group_size)
    slab_width = kv_here * 2 * HD
    score_scale = HD ** (-0.5)
    head_map = np.arange(heads_here) // group_size
    dest_table = (
        np.arange(tp_count)[:, None] * heads_here // group_size + np.arange(kv_here)[None, :]
    ).reshape(-1)
    routed = jnp.take(suffix_states, request_order, axis=0)
    routed_here = lax.all_to_all(routed, "dp", split_axis=0, concat_axis=1, tiled=True)
    width_here = routed_here.shape[2]
    state_shard = routed_here.reshape(row_count, width_here)
    slot_ids = dp_index * local_reqs + jnp.arange(local_reqs, dtype=jnp.int32)
    req_ids = jnp.take(request_order, slot_ids)
    lengths_here = jnp.take(suffix_lengths, req_ids)
    owner_here = jnp.take(group_owner, jnp.take(request_group[:, 0], req_ids))
    position = jnp.arange(L_MAX, dtype=jnp.int32)
    valid = (position[None, :] < lengths_here[:, None]).reshape(row_count)
    positions = (P_SIZE + jnp.tile(position, local_reqs)).astype(jnp.float32)
    full_rows = lax.all_gather(state_shard, "tensor", axis=1, tiled=True)
    normed = rms_scale(full_rows, norm_attn)
    query = rotate(
        jnp.dot(normed, w_query, preferred_element_type=jnp.float32).reshape(
            row_count, heads_here, HD
        ),
        positions,
    ).astype(jnp.bfloat16)
    key_part = jnp.dot(normed, w_key, preferred_element_type=jnp.float32).astype(jnp.bfloat16)
    value_part = jnp.dot(normed, w_value, preferred_element_type=jnp.float32).astype(jnp.bfloat16)
    key_full, value_full = (
        lax.all_gather(key_part, "tensor", axis=1, tiled=True),
        lax.all_gather(value_part, "tensor", axis=1, tiled=True),
    )
    key_heads = key_full.reshape(row_count, HD, KVH).transpose(0, 2, 1)
    value_heads = value_full.reshape(row_count, HD, KVH).transpose(0, 2, 1)
    key_rot = rotate(key_heads.astype(jnp.float32), positions).astype(jnp.bfloat16)
    cache_width = key_part.shape[1]
    keys_flat = jnp.where(valid[:, None], key_rot.reshape(row_count, KVH * HD), 0.0)
    values_flat = jnp.where(valid[:, None], value_heads.reshape(row_count, KVH * HD), 0.0)
    keys_out = lax.dynamic_slice_in_dim(keys_flat, tp_index * cache_width, cache_width, 1).reshape(
        local_reqs, L_MAX, cache_width
    )
    values_out = lax.dynamic_slice_in_dim(
        values_flat, tp_index * cache_width, cache_width, 1
    ).reshape(local_reqs, L_MAX, cache_width)
    kv_first = tp_index * heads_here // group_size
    own_keys = lax.dynamic_slice_in_dim(key_rot, kv_first, kv_here, 1)[:, head_map].reshape(
        local_reqs, L_MAX, heads_here, HD
    )
    own_values = lax.dynamic_slice_in_dim(value_heads, kv_first, kv_here, 1)[:, head_map].reshape(
        local_reqs, L_MAX, heads_here, HD
    )
    query_req = query.reshape(local_reqs, L_MAX, heads_here, HD)

    def absorb_prefix(state_one, query_one, slot_block):
        block = slot_block.reshape(slot_block.shape[0], kv_here, 2, HD)
        key_rows = block[:, head_map, 0]
        value_rows = block[:, head_map, 1]
        scores = (
            jnp.einsum("thd,phd->htp", query_one, key_rows, preferred_element_type=jnp.float32)
            * score_scale
        )
        return absorb_block(state_one, scores, jnp.ones((1, 1, 1), bool), value_rows)

    initial = tuple(
        (
            (
                jnp.full((heads_here, L_MAX), -1e30, jnp.float32),
                jnp.zeros((heads_here, L_MAX), jnp.float32),
                jnp.zeros((heads_here, L_MAX, HD), jnp.float32),
            )
            for request in range(local_reqs)
        )
    )
    all_rows = lax.all_gather(prefix_cache, "dp", axis=0, tiled=True)
    rows_each = all_rows.shape[1]
    chosen = jnp.take(all_rows.reshape(dp_count, rows_each, KVH, 2 * HD), dest_table, axis=2)
    picked = lax.all_to_all(chosen, "tensor", split_axis=2, concat_axis=1, tiled=True).reshape(
        dp_count, P_SIZE, slab_width
    )
    states = tuple(
        (
            absorb_prefix(
                initial[request],
                query_req[request],
                lax.dynamic_index_in_dim(picked, owner_here[request], 0, keepdims=False),
            )
            for request in range(local_reqs)
        )
    )
    pieces = []
    for request in range(local_reqs):
        self_scores = (
            jnp.einsum(
                "thd,shd->hts",
                query_req[request],
                own_keys[request],
                preferred_element_type=jnp.float32,
            )
            * score_scale
        )
        self_allowed = (position[None, :] <= position[:, None]) & (
            position[None, :] < lengths_here[request]
        )
        running_max, running_sum, numerator = absorb_block(
            states[request], self_scores, self_allowed[None], own_values[request]
        )
        attention_one = (numerator / running_sum[:, :, None]).astype(jnp.bfloat16)
        pieces.append(attention_one.transpose(1, 0, 2).reshape(L_MAX, heads_here * HD))
    attention = jnp.concatenate(pieces, axis=0)
    attn_terms = jnp.dot(attention, w_out, preferred_element_type=jnp.float32)
    attn_share = lax.psum_scatter(
        attn_terms.astype(jnp.bfloat16), "tensor", scatter_dimension=1, tiled=True
    ).astype(jnp.float32)
    middle = (state_shard.astype(jnp.float32) + attn_share).astype(jnp.bfloat16)
    middle_rows = lax.all_gather(middle, "tensor", axis=1, tiled=True)
    normed_two = rms_scale(middle_rows, norm_mlp)
    gate = jnp.dot(normed_two, w_gate, preferred_element_type=jnp.float32)
    upper = jnp.dot(normed_two, w_up, preferred_element_type=jnp.float32)
    hidden = (jax.nn.silu(gate) * upper).astype(jnp.bfloat16)
    down_terms = jnp.dot(hidden, w_down, preferred_element_type=jnp.float32)
    down_share = lax.psum_scatter(
        down_terms.astype(jnp.bfloat16), "tensor", scatter_dimension=1, tiled=True
    ).astype(jnp.float32)
    result = middle.astype(jnp.float32) + down_share
    result = (
        jnp.where(valid[:, None], result, 0.0)
        .astype(jnp.bfloat16)
        .reshape(local_reqs, L_MAX, width_here)
    )
    returned = lax.all_to_all(result, "dp", split_axis=1, concat_axis=0, tiled=True)
    hidden_out = jnp.zeros_like(returned).at[request_order].set(returned)
    return (hidden_out, keys_out, values_out)


def solution(mesh):
    in_specs = (
        P(None, "dp", "tensor"),
        P(),
        P(),
        P(),
        P(),
        P("dp", "tensor", None),
        P(),
        P(None, "tensor"),
        P(None, "tensor"),
        P(None, "tensor"),
        P("tensor", None),
        P(),
        P(None, "tensor"),
        P(None, "tensor"),
        P("tensor", None),
    )
    out_specs = (P(None, "dp", "tensor"), P("dp", None, "tensor"), P("dp", None, "tensor"))
    return jax.shard_map(shards, mesh=mesh, in_specs=in_specs, out_specs=out_specs, check_vma=False)
```

profile of v0, /device:TPU:8, one launch (start us, length us, event | category | flops | bytes accessed | tf_op | source)
XLA Modules:
  0.0 635.4 jit_solution(12212164289237570744)
XLA Ops:
  7.2 0.7 compare_select_fusion.3
  7.9 0.7 compare_and_fusion.1
  8.6 1.4 gather_fusion
  10.1 0.7 reshape.707
  10.9 16.0 %all-to-all-start = ((bf16[16,2,512]{2,1,0:T(2,128)(2,1)}), bf16[16,2,512]{2,1,0:T(2,128)(2,1)S(1)}, u32[]{:S(2)}, u32[]{:S(2)}) async-start(bf16[16,2,512]{2,1,0:T(2,128)(2,1)} %reshape.707), calls=%async_computation | async-start | bytes 65536 | tf_op jit(solution)/shard_map/all_to_all | solution.py:82
  26.9 49.1 %all_gather.16 = bf16[16,8,1024]{2,1,0:T(8,128)(2,1)S(1)} all-gather(bf16[1,8,1024]{2,1,0:T(8,128)(2,1)} %param.30), channel_id=1, replica_groups=mesh['dp'=16,'tensor'=32] {'dp'}, dimensions={0}, use_global_device_ids=true | all-gather | bytes 278528 | tf_op jit(solution)/shard_map/all_gather | solution.py:147
  76.0 0.7 pad_clamp_fusion.1
  76.7 1.9 gather_fusion.1
  78.6 6.7 %all-to-all-start.1 = ((bf16[16,8,32,128]{3,1,0,2:T(8,128)(2,1)}), bf16[16,8,32,128]{3,1,0,2:T(8,128)(2,1)S(1)}, u32[]{:S(2)}, u32[]{:S(2)}) async-start(bf16[16,8,32,128]{3,1,0,2:T(8,128)(2,1)} %bitcast.9), calls=%async_computation.1 | async-start | bytes 2097152 | tf_op jit(solution)/shard_map/all_to_all | solution.py:150
  85.4 0.6 gather_fusion.3
  86.1 0.7 copy.51
  87.0 0.6 gather_fusion.5
  87.6 0.6 gather_fusion.4
  88.3 0.6 gather_fusion.2
  88.9 0.6 fusion.81
  93.5 0.6 fusion.80
  94.1 0.6 iota_compare_fusion.2
  94.7 0.7 iota_compare_fusion.1
  95.6 17.5 %all-to-all-done.1 = bf16[16,8,32,128]{3,1,0,2:T(8,128)(2,1)S(1)} async-done(((bf16[16,8,32,128]{3,1,0,2:T(8,128)(2,1)}), bf16[16,8,32,128]{3,1,0,2:T(8,128)(2,1)S(1)}, u32[]{:S(2)}, u32[]{:S(2)}) %all-to-all-start.1) | async-done | bytes 1048608 | tf_op jit(solution)/shard_map/all_to_all | solution.py:150
  113.1 0.3 copy_bitcast_fusion
  113.6 37.2 %all-gather.3.cloned.1.call-done = bf16[256,2048]{0,1:T(8,128)(2,1)} async-done(((bf16[256,64]{0,1:T(8,128)(2,1)}), bf16[256,2048]{0,1:T(8,128)(2,1)}) %all-gather.3.cloned.1.call-update) | async-done | bytes 1048592 | tf_op jit(solution)/shard_map/all_gather | solution.py:92
  150.8 1.6 fusion
  152.5 0.5 convolution_bitcast_fusion
  153.3 0.5 convolution_convert_fusion.2
  153.8 41.5 %all_gather.18 = bf16[256,512]{0,1:T(8,128)(2,1)S(1)} all-gather(bf16[256,16]{0,1:T(8,128)(2,1)S(1)} %convolution_convert_fusion.2), channel_id=1, replica_groups=mesh['dp'=16,'tensor'=32] {'tensor'}, dimensions={1}, use_global_device_ids=true | all-gather | bytes 270336 | tf_op jit(solution)/shard_map/all_gather | solution.py:104
  195.4 0.5 convolution_convert_fusion.3
  195.8 38.9 %all_gather.17 = bf16[256,512]{0,1:T(8,128)(2,1)S(1)} all-gather(bf16[256,16]{0,1:T(8,128)(2,1)S(1)} %convolution_convert_fusion.3), channel_id=1, replica_groups=mesh['dp'=16,'tensor'=32] {'tensor'}, dimensions={1}, use_global_device_ids=true | all-gather | bytes 270336 | tf_op jit(solution)/shard_map/all_gather | solution.py:103
  235.0 0.3 fusion.82
  235.2 0.3 fusion.83
  235.7 0.2 select_reduce_fusion.1
  235.9 0.2 select_reduce_fusion
  237.0 0.2 fusion.10
  237.2 0.2 fusion.12
  237.7 1.5 convolution_convert_fusion.1
  239.2 147.1 %reduce-scatter.3.cloned.1.call-done = bf16[256,64]{0,1:T(8,128)(2,1)} async-done(((bf16[256,2048]{0,1:T(8,128)(2,1)}), bf16[256,64]{0,1:T(8,128)(2,1)}) %reduce-scatter.3.cloned.1.call-update) | async-done | bytes 32784 | tf_op jit(solution)/shard_map/reduce_scatter | solution.py:184
  386.3 1.4 add_convert_fusion
  387.8 59.3 %all-gather.5.cloned.1.call-done = bf16[256,2048]{0,1:T(8,128)(2,1)} async-done(((bf16[256,64]{0,1:T(8,128)(2,1)}), bf16[256,2048]{0,1:T(8,128)(2,1)}) %all-gather.5.cloned.1.call-update) | async-done | bytes 1048592 | tf_op jit(solution)/shard_map/all_gather | solution.py:188
  447.1 1.6 fusion.3
  448.8 2.1 fusion.15
  450.9 4.1 convolution_convert_fusion
  455.1 148.5 %reduce-scatter.5.cloned.1.call-done = bf16[256,64]{0,1:T(8,128)(2,1)} async-done(((bf16[256,2048]{0,1:T(8,128)(2,1)}), bf16[256,64]{0,1:T(8,128)(2,1)}) %reduce-scatter.5.cloned.1.call-update) | async-done | bytes 32784 | tf_op jit(solution)/shard_map/reduce_scatter | solution.py:194
  603.6 0.8 select_convert_fusion
  604.5 0.7 reshape.709
  605.2 10.2 %all-to-all-start.2 = ((bf16[16,2,512]{2,1,0:T(2,128)(2,1)}), bf16[16,2,512]{2,1,0:T(2,128)(2,1)S(1)}, u32[]{:S(2)}, u32[]{:S(2)}) async-start(bf16[16,2,512]{2,1,0:T(2,128)(2,1)} %reshape.709), calls=%async_computation.4 | async-start | bytes 65536 | tf_op jit(solution)/shard_map/all_to_all | solution.py:203
  615.4 0.6 copy_bitcast_fusion.3
  616.0 10.5 %all-to-all-done.2 = bf16[16,2,512]{2,1,0:T(2,128)(2,1)S(1)} async-done(((bf16[16,2,512]{2,1,0:T(2,128)(2,1)}), bf16[16,2,512]{2,1,0:T(2,128)(2,1)S(1)}, u32[]{:S(2)}, u32[]{:S(2)}) %all-to-all-start.2) | async-done | bytes 32800 | tf_op jit(solution)/shard_map/all_to_all | solution.py:203
  626.8 1.5 scatter_fusion
  628.3 0.6 copy-done.9
  (85 shorter events, 3.1 us)
Async XLA Ops:
  7.2 443.7 %copy-start = (bf16[256,2048]{1,0:T(8,128)(2,1)S(1)}, bf16[256,2048]{1,0:T(8,128)(2,1)}, u32[]{:S(2)}) copy-start(bf16[256,2048]{1,0:T(8,128)(2,1)} %param.39) | copy-start | bytes 3145732
  10.9 67.7 %all-to-all-start = ((bf16[16,2,512]{2,1,0:T(2,128)(2,1)}), bf16[16,2,512]{2,1,0:T(2,128)(2,1)S(1)}, u32[]{:S(2)}, u32[]{:S(2)}) async-start(bf16[16,2,512]{2,1,0:T(2,128)(2,1)} %reshape.707), calls=%async_computation | async-start | bytes 65536 | tf_op jit(solution)/shard_map/all_to_all | solution.py:82
  78.6 6.8 %copy-start.1 = (s32[32]{0:T(128)S(1)}, s32[32]{0:T(128)}, u32[]{:S(2)}) copy-start(s32[32]{0:T(128)} %param.29) | copy-start | bytes 388
  78.6 8.4 %copy-start.2 = (s32[32,1]{0,1:T(1,128)S(1)}, s32[32,1]{0,1:T(1,128)}, u32[]{:S(2)}) copy-start(s32[32,1]{0,1:T(1,128)} %param.27) | copy-start | bytes 388
  78.6 34.5 %all-to-all-start.1 = ((bf16[16,8,32,128]{3,1,0,2:T(8,128)(2,1)}), bf16[16,8,32,128]{3,1,0,2:T(8,128)(2,1)S(1)}, u32[]{:S(2)}, u32[]{:S(2)}) async-start(bf16[16,8,32,128]{3,1,0,2:T(8,128)(2,1)} %bitcast.9), calls=%async_computation.1 | async-start | bytes 2097152 | tf_op jit(solution)/shard_map/all_to_all | solution.py:150
  85.3 2.4 copy-start.3
  85.3 3.0 copy-start.4
  85.3 65.6 %all-gather.3.cloned.1.call-start = ((), (), s32[]{:S(2)}) async-start(), calls=%async_computation.5 | async-start | bytes 1081344 | tf_op jit(solution)/shard_map/all_gather | solution.py:92
  86.0 6.1 copy-start.11
  86.9 299.5 %reduce-scatter.3.cloned.1.call-start = ((), (), s32[]{:S(2)}) async-start(), calls=%async_computation.6 | async-start | bytes 1081344 | tf_op jit(solution)/shard_map/reduce_scatter | solution.py:184
  113.4 39.1 %copy-start.13 = (bf16[2048,64]{0,1:T(8,128)(2,1)S(1)}, bf16[2048,64]{0,1:T(8,128)(2,1)}, u32[]{:S(2)}) copy-start(bf16[2048,64]{0,1:T(8,128)(2,1)} %param.32) | copy-start | bytes 786436
  150.8 1.6 copy-start.5
  152.5 0.8 copy-start.14
  153.3 42.0 %copy-start.15 = (bf16[2048,16]{0,1:T(8,128)(2,1)S(1)}, bf16[2048,16]{0,1:T(8,128)(2,1)}, u32[]{:S(2)}) copy-start(bf16[2048,16]{0,1:T(8,128)(2,1)} %param.33) | copy-start | bytes 196612
  235.6 2.1 copy-start.10
  237.7 148.7 %copy-start.7 = (bf16[256,64]{0,1:T(8,128)(2,1)S(1)}, bf16[256,64]{0,1:T(8,128)(2,1)}, u32[]{:S(2)}) copy-start(bf16[256,64]{0,1:T(8,128)(2,1)} %copy.51) | copy-start | bytes 98308
  237.7 150.1 %copy-start.12 = (bf16[2048]{0:T(1024)(128)(2,1)S(1)}, bf16[2048]{0:T(1024)(128)(2,1)}, u32[]{:S(2)}) copy-start(bf16[2048]{0:T(1024)(128)(2,1)} %param.36) | copy-start | bytes 12292
  239.2 207.9 %all-gather.5.cloned.1.call-start = ((), (), s32[]{:S(2)}) async-start(), calls=%async_computation.7 | async-start | bytes 1081344 | tf_op jit(solution)/shard_map/all_gather | solution.py:188
  387.7 215.8 %reduce-scatter.5.cloned.1.call-start = ((), (), s32[]{:S(2)}) async-start(), calls=%async_computation.8 | async-start | bytes 1081344 | tf_op jit(solution)/shard_map/reduce_scatter | solution.py:194
  447.1 1.6 copy-start.6
  454.9 148.7 %copy-start.8 = (bf16[256,64]{0,1:T(8,128)(2,1)S(1)}, bf16[256,64]{0,1:T(8,128)(2,1)}, u32[]{:S(2)}) copy-start(bf16[256,64]{0,1:T(8,128)(2,1)} %add_convert_fusion) | copy-start | bytes 98308
  605.2 21.4 %all-to-all-start.2 = ((bf16[16,2,512]{2,1,0:T(2,128)(2,1)}), bf16[16,2,512]{2,1,0:T(2,128)(2,1)S(1)}, u32[]{:S(2)}, u32[]{:S(2)}) async-start(bf16[16,2,512]{2,1,0:T(2,128)(2,1)} %reshape.709), calls=%async_computation.4 | async-start | bytes 65536 | tf_op jit(solution)/shard_map/all_to_all | solution.py:203
  628.3 0.6 copy-start.9
Sparse Core Ops, SparseCore 0:
  88.8 61.9 all-gather.2
  239.3 146.9 reduce-scatter.2
  389.1 58.0 all-gather.4
  455.1 148.4 reduce-scatter.4
where the time goes:
time: 636 us; the launch traced here: 635 us
  waiting for transfers between devices  420 us (66%)
  blocking collectives  130 us (20%)
  starting transfers between devices  33.1 us (5%)
  between operations  18.1 us (3%)
  local copies, waits for them, and re-layouts  13.2 us (2%)
  matrix products  11 us (2%)
  other arithmetic  10.2 us (2%)
    reduce_scatter x1, waiting for transfers between devices, shards(): lax.psum_scatter(down_terms.astype(jnp.bfloat16), 'tensor', scatter_dimen...  149 us
    reduce_scatter x1, waiting for transfers between devices, shards(): lax.psum_scatter(attn_terms.astype(jnp.bfloat16), 'tensor', scatter_dimen...  147 us
    all_gather x1, waiting for transfers between devices, shards(): middle_rows = lax.all_gather(middle, 'tensor', axis=1, tiled=True)  59.3 us
    all_gather x1, blocking collectives, shards(): all_rows = lax.all_gather(prefix_cache, 'dp', axis=0, tiled=True)  49.1 us
    all_gather x1, blocking collectives, shards(): lax.all_gather(value_part, 'tensor', axis=1, tiled=True)  41.5 us
    all_gather x1, blocking collectives, shards(): lax.all_gather(key_part, 'tensor', axis=1, tiled=True)  38.9 us
    all_gather x1, waiting for transfers between devices, shards(): full_rows = lax.all_gather(state_shard, 'tensor', axis=1, tiled=True)  37.2 us
    all_to_all x1, waiting for transfers between devices, shards(): lax.all_to_all(chosen, 'tensor', split_axis=2, concat_axis=1, tiled=True)  17.5 us
  transfers between devices with their start and end apart: 7, of which 6 were waited for; matrix products, arithmetic and copies ran while one was open for 2% of the time, Pallas kernels for 0%

commit v1 on v0

--- a/solution.py
+++ b/solution.py
@@ -144,7 +144,10 @@
             for request in range(local_reqs)
         )
     )
-    all_rows = lax.all_gather(prefix_cache, "dp", axis=0, tiled=True)
+    view_out = lax.axis_size("dp")
+    f_next = jnp.stack(view_out * [prefix_cache], 0)
+    local_part = lax.all_to_all(f_next, "dp", 0, 0)
+    all_rows = jnp.concatenate(local_part, 0)
     rows_each = all_rows.shape[1]
     chosen = jnp.take(all_rows.reshape(dp_count, rows_each, KVH, 2 * HD), dest_table, axis=2)
     picked = lax.all_to_all(chosen, "tensor", split_axis=2, concat_axis=1, tiled=True).reshape(

time: 636 us -> 601 us (0.945)
  blocking collectives: 130 us -> 80.2 us
  waiting for transfers between devices: 420 us -> 428 us
    all_gather x1 -> x0, blocking collectives: 49.1 us -> none  [shards(): all_rows = lax.all_gather(prefix_cache, 'dp', axis=0, tiled=True)]
    all_to_all x1, waiting for transfers between devices: 17.5 us -> 0.01 us  [shards(): lax.all_to_all(chosen, 'tensor', split_axis=2, concat_axis=1, tiled=True)]
    all_to_all x1, waiting for transfers between devices: 0.01 us -> 11.2 us  [shards(): lax.all_to_all(routed, 'dp', split_axis=0, concat_axis=1, tiled=True)]
    all_gather x1, waiting for transfers between devices: 37.2 us -> 47.9 us  [shards(): full_rows = lax.all_gather(state_shard, 'tensor', axis=1, tiled=True)]
  transfers between devices with their start and end apart: 7 -> 8, of which waited for: 6 -> 7; matrix products, arithmetic and copies ran while one was open for 2% -> 2% of each run, Pallas kernels for 0% -> 0%
where the time goes in v1:
time: 601 us; the launch traced here: 600 us
  waiting for transfers between devices  428 us (71%)
  blocking collectives  80.2 us (13%)
  starting transfers between devices  38.5 us (6%)
  between operations  18.1 us (3%)
  local copies, waits for them, and re-layouts  15.3 us (3%)
  matrix products  11 us (2%)
  other arithmetic  9.54 us (2%)
    reduce_scatter x1, waiting for transfers between devices, shards(): lax.psum_scatter(down_terms.astype(jnp.bfloat16), 'tensor', scatter_dimen...  149 us
    reduce_scatter x1, waiting for transfers between devices, shards(): lax.psum_scatter(attn_terms.astype(jnp.bfloat16), 'tensor', scatter_dimen...  147 us
    all_gather x1, waiting for transfers between devices, shards(): middle_rows = lax.all_gather(middle, 'tensor', axis=1, tiled=True)  59.7 us
    all_gather x1, waiting for transfers between devices, shards(): full_rows = lax.all_gather(state_shard, 'tensor', axis=1, tiled=True)  47.9 us
    all_gather x1, blocking collectives, shards(): lax.all_gather(value_part, 'tensor', axis=1, tiled=True)  41.2 us
    all_gather x1, blocking collectives, shards(): lax.all_gather(key_part, 'tensor', axis=1, tiled=True)  38.9 us
    all_to_all x1, starting transfers between devices, shards(): lax.all_to_all(routed, 'dp', split_axis=0, concat_axis=1, tiled=True)  16 us
  transfers between devices with their start and end apart: 8, of which 7 were waited for; matrix products, arithmetic and copies ran while one was open for 2% of the time, Pallas kernels for 0%

profile of v1, /device:TPU:8, one launch (start us, length us, event | category | flops | bytes accessed | tf_op | source)
XLA Modules:
  0.0 600.2 jit_solution(7727691670454854566)
XLA Ops:
  7.2 0.8 compare_select_fusion.3
  7.9 0.7 compare_and_fusion.1
  8.6 1.4 gather_fusion
  10.2 0.7 reshape.706
  10.9 16.0 %all-to-all-start = ((bf16[16,2,512]{2,1,0:T(2,128)(2,1)}), bf16[16,2,512]{2,1,0:T(2,128)(2,1)S(1)}, u32[]{:S(2)}, u32[]{:S(2)}) async-start(bf16[16,2,512]{2,1,0:T(2,128)(2,1)} %reshape.706), calls=%async_computation | async-start | bytes 65536 | tf_op jit(solution)/shard_map/all_to_all | solution.py:82
  26.9 11.2 %all-to-all-done = bf16[16,2,512]{2,1,0:T(2,128)(2,1)S(1)} async-done(((bf16[16,2,512]{2,1,0:T(2,128)(2,1)}), bf16[16,2,512]{2,1,0:T(2,128)(2,1)S(1)}, u32[]{:S(2)}, u32[]{:S(2)}) %all-to-all-start) | async-done | bytes 32800 | tf_op jit(solution)/shard_map/all_to_all | solution.py:82
  38.1 1.5 stack.2
  39.5 4.8 all-to-all-start.1
  44.5 0.7 copy.51
  45.3 0.6 gather_fusion.3
  46.0 0.6 gather_fusion.5
  46.6 0.6 gather_fusion.4
  47.3 0.6 gather_fusion.2
  48.0 0.7 fusion.80
  48.6 0.6 iota_compare_fusion.2
  49.3 0.6 fusion.81
  49.9 0.6 iota_compare_fusion.1
  54.7 2.9 all-to-all-done.1
  57.6 1.9 gather_fusion.1
  59.5 7.4 %all-to-all-start.2 = ((bf16[16,8,32,128]{3,1,0,2:T(8,128)(2,1)}), bf16[16,8,32,128]{3,1,0,2:T(8,128)(2,1)S(1)}, u32[]{:S(2)}, u32[]{:S(2)}) async-start(bf16[16,8,32,128]{3,1,0,2:T(8,128)(2,1)} %bitcast.10), calls=%async_computation.2 | async-start | bytes 2097152 | tf_op jit(solution)/shard_map/all_to_all | solution.py:153
  66.9 47.9 %all-gather.3.cloned.1.call-done = bf16[256,2048]{0,1:T(8,128)(2,1)} async-done(((bf16[256,64]{0,1:T(8,128)(2,1)}), bf16[256,2048]{0,1:T(8,128)(2,1)}) %all-gather.3.cloned.1.call-update) | async-done | bytes 1048592 | tf_op jit(solution)/shard_map/all_gather | solution.py:92
  114.8 1.6 fusion
  116.4 0.5 convolution_convert_fusion.2
  116.9 41.2 %all_gather.14 = bf16[256,512]{0,1:T(8,128)(2,1)S(1)} all-gather(bf16[256,16]{0,1:T(8,128)(2,1)S(1)} %convolution_convert_fusion.2), channel_id=1, replica_groups=mesh['dp'=16,'tensor'=32] {'tensor'}, dimensions={1}, use_global_device_ids=true | all-gather | bytes 270336 | tf_op jit(solution)/shard_map/all_gather | solution.py:104
  158.2 0.5 convolution_convert_fusion.3
  158.6 38.9 %all_gather.13 = bf16[256,512]{0,1:T(8,128)(2,1)S(1)} all-gather(bf16[256,16]{0,1:T(8,128)(2,1)S(1)} %convolution_convert_fusion.3), channel_id=1, replica_groups=mesh['dp'=16,'tensor'=32] {'tensor'}, dimensions={1}, use_global_device_ids=true | all-gather | bytes 270336 | tf_op jit(solution)/shard_map/all_gather | solution.py:103
  197.9 0.7 copy-done.14
  198.6 0.5 convolution_bitcast_fusion
  199.3 0.2 select_reduce_fusion.1
  199.5 0.2 select_reduce_fusion
  199.8 0.3 copy_bitcast_fusion
  200.3 0.3 fusion.82
  200.6 0.3 fusion.83
  202.4 1.5 convolution_convert_fusion.1
  204.0 146.8 %reduce-scatter.3.cloned.1.call-done = bf16[256,64]{0,1:T(8,128)(2,1)} async-done(((bf16[256,2048]{0,1:T(8,128)(2,1)}), bf16[256,64]{0,1:T(8,128)(2,1)}) %reduce-scatter.3.cloned.1.call-update) | async-done | bytes 32784 | tf_op jit(solution)/shard_map/reduce_scatter | solution.py:187
  350.7 1.4 add_convert_fusion
  352.2 59.7 %all-gather.5.cloned.1.call-done = bf16[256,2048]{0,1:T(8,128)(2,1)} async-done(((bf16[256,64]{0,1:T(8,128)(2,1)}), bf16[256,2048]{0,1:T(8,128)(2,1)}) %all-gather.5.cloned.1.call-update) | async-done | bytes 1048592 | tf_op jit(solution)/shard_map/all_gather | solution.py:191
  411.9 1.6 fusion.3
  413.6 2.1 fusion.15
  415.6 4.1 convolution_convert_fusion
  419.8 148.5 %reduce-scatter.5.cloned.1.call-done = bf16[256,64]{0,1:T(8,128)(2,1)} async-done(((bf16[256,2048]{0,1:T(8,128)(2,1)}), bf16[256,64]{0,1:T(8,128)(2,1)}) %reduce-scatter.5.cloned.1.call-update) | async-done | bytes 32784 | tf_op jit(solution)/shard_map/reduce_scatter | solution.py:197
  568.4 0.8 select_convert_fusion
  569.3 0.7 reshape.708
  570.0 10.1 %all-to-all-start.3 = ((bf16[16,2,512]{2,1,0:T(2,128)(2,1)}), bf16[16,2,512]{2,1,0:T(2,128)(2,1)S(1)}, u32[]{:S(2)}, u32[]{:S(2)}) async-start(bf16[16,2,512]{2,1,0:T(2,128)(2,1)} %reshape.708), calls=%async_computation.5 | async-start | bytes 65536 | tf_op jit(solution)/shard_map/all_to_all | solution.py:206
  580.2 0.6 copy_bitcast_fusion.3
  580.8 10.5 %all-to-all-done.3 = bf16[16,2,512]{2,1,0:T(2,128)(2,1)S(1)} async-done(((bf16[16,2,512]{2,1,0:T(2,128)(2,1)}), bf16[16,2,512]{2,1,0:T(2,128)(2,1)S(1)}, u32[]{:S(2)}, u32[]{:S(2)}) %all-to-all-start.3) | async-done | bytes 32800 | tf_op jit(solution)/shard_map/all_to_all | solution.py:206
  591.5 1.5 scatter_fusion
  593.0 0.6 copy-done.9
  (89 shorter events, 3.5 us)
Async XLA Ops:
  7.2 408.5 %copy-start = (bf16[256,2048]{1,0:T(8,128)(2,1)S(1)}, bf16[256,2048]{1,0:T(8,128)(2,1)}, u32[]{:S(2)}) copy-start(bf16[256,2048]{1,0:T(8,128)(2,1)} %param.39) | copy-start | bytes 3145732
  7.2 38.1 %copy-start.1 = (s32[32]{0:T(128)S(1)}, s32[32]{0:T(128)}, u32[]{:S(2)}) copy-start(s32[32]{0:T(128)} %param.29) | copy-start | bytes 388
  8.6 37.4 %copy-start.2 = (s32[32,1]{0,1:T(1,128)S(1)}, s32[32,1]{0,1:T(1,128)}, u32[]{:S(2)}) copy-start(s32[32,1]{0,1:T(1,128)} %param.27) | copy-start | bytes 388
  10.9 27.2 %all-to-all-start = ((bf16[16,2,512]{2,1,0:T(2,128)(2,1)}), bf16[16,2,512]{2,1,0:T(2,128)(2,1)S(1)}, u32[]{:S(2)}, u32[]{:S(2)}) async-start(bf16[16,2,512]{2,1,0:T(2,128)(2,1)} %reshape.706), calls=%async_computation | async-start | bytes 65536 | tf_op jit(solution)/shard_map/all_to_all | solution.py:82
  39.5 7.1 %copy-start.3 = (s32[32]{0:T(128)S(1)}, s32[32]{0:T(128)}, u32[]{:S(2)}) copy-start(s32[32]{0:T(128)} %param.26) | copy-start | bytes 388
  39.5 18.1 %all-to-all-start.1 = ((bf16[16,1,8,1024]{3,2,1,0:T(8,128)(2,1)}), bf16[16,1,8,1024]{3,2,1,0:T(8,128)(2,1)S(1)}, u32[]{:S(2)}, u32[]{:S(2)}) async-start(bf16[16,1,8,1024]{3,2,1,0:T(8,128)(2,1)} %stack.2), calls=%async_computation.1 | async-start | bytes 524288 | tf_op jit(solution)/shard_map/all_to_all | solution.py:149
  44.3 3.0 copy-start.4
  44.3 70.4 %all-gather.3.cloned.1.call-start = ((), (), s32[]{:S(2)}) async-start(), calls=%async_computation.6 | async-start | bytes 1081344 | tf_op jit(solution)/shard_map/all_gather | solution.py:92
  45.3 7.8 %copy-start.11 = (bf16[2048]{0:T(1024)(128)(2,1)S(1)}, bf16[2048]{0:T(1024)(128)(2,1)}, u32[]{:S(2)}) copy-start(bf16[2048]{0:T(1024)(128)(2,1)} %param.31) | copy-start | bytes 12292
  45.3 9.1 %copy-start.13 = (s32[32]{0:T(128)S(1)}, s32[32]{0:T(128)}, u32[]{:S(2)}) copy-start(s32[32]{0:T(128)} %constant.238) | copy-start | bytes 388
  59.5 56.9 %copy-start.15 = (bf16[2048,16]{0,1:T(8,128)(2,1)S(1)}, bf16[2048,16]{0,1:T(8,128)(2,1)}, u32[]{:S(2)}) copy-start(bf16[2048,16]{0,1:T(8,128)(2,1)} %param.34) | copy-start | bytes 196612
  59.5 140.3 %all-to-all-start.2 = ((bf16[16,8,32,128]{3,1,0,2:T(8,128)(2,1)}), bf16[16,8,32,128]{3,1,0,2:T(8,128)(2,1)S(1)}, u32[]{:S(2)}, u32[]{:S(2)}) async-start(bf16[16,8,32,128]{3,1,0,2:T(8,128)(2,1)} %bitcast.10), calls=%async_computation.2 | async-start | bytes 2097152 | tf_op jit(solution)/shard_map/all_to_all | solution.py:153
  66.9 283.9 %reduce-scatter.3.cloned.1.call-start = ((), (), s32[]{:S(2)}) async-start(), calls=%async_computation.7 | async-start | bytes 1081344 | tf_op jit(solution)/shard_map/reduce_scatter | solution.py:187
  114.8 1.6 copy-start.5
  116.4 41.8 %copy-start.16 = (bf16[2048,16]{0,1:T(8,128)(2,1)S(1)}, bf16[2048,16]{0,1:T(8,128)(2,1)}, u32[]{:S(2)}) copy-start(bf16[2048,16]{0,1:T(8,128)(2,1)} %param.33) | copy-start | bytes 196612
  197.6 1.0 copy-start.14
  200.1 2.4 copy-start.10
  202.4 148.3 %copy-start.7 = (bf16[256,64]{0,1:T(8,128)(2,1)S(1)}, bf16[256,64]{0,1:T(8,128)(2,1)}, u32[]{:S(2)}) copy-start(bf16[256,64]{0,1:T(8,128)(2,1)} %copy.51) | copy-start | bytes 98308
  202.4 149.8 %copy-start.12 = (bf16[2048]{0:T(1024)(128)(2,1)S(1)}, bf16[2048]{0:T(1024)(128)(2,1)}, u32[]{:S(2)}) copy-start(bf16[2048]{0:T(1024)(128)(2,1)} %param.36) | copy-start | bytes 12292
  203.9 208.0 %all-gather.5.cloned.1.call-start = ((), (), s32[]{:S(2)}) async-start(), calls=%async_computation.8 | async-start | bytes 1081344 | tf_op jit(solution)/shard_map/all_gather | solution.py:191
  352.1 216.2 %reduce-scatter.5.cloned.1.call-start = ((), (), s32[]{:S(2)}) async-start(), calls=%async_computation.9 | async-start | bytes 1081344 | tf_op jit(solution)/shard_map/reduce_scatter | solution.py:197
  411.9 1.6 copy-start.6
  419.7 148.7 %copy-start.8 = (bf16[256,64]{0,1:T(8,128)(2,1)S(1)}, bf16[256,64]{0,1:T(8,128)(2,1)}, u32[]{:S(2)}) copy-start(bf16[256,64]{0,1:T(8,128)(2,1)} %add_convert_fusion) | copy-start | bytes 98308
  570.0 21.3 %all-to-all-start.3 = ((bf16[16,2,512]{2,1,0:T(2,128)(2,1)}), bf16[16,2,512]{2,1,0:T(2,128)(2,1)S(1)}, u32[]{:S(2)}, u32[]{:S(2)}) async-start(bf16[16,2,512]{2,1,0:T(2,128)(2,1)} %reshape.708), calls=%async_computation.5 | async-start | bytes 65536 | tf_op jit(solution)/shard_map/all_to_all | solution.py:206
  593.0 0.6 copy-start.9
Sparse Core Ops, SparseCore 0:
  47.9 66.8 all-gather.2
  204.1 146.6 reduce-scatter.2
  353.5 58.4 all-gather.4
  419.9 148.4 reduce-scatter.4
